TPU v7x, 512 devices: a whole 4x4x16 slice. The times are simulated.
512 devices in a mesh: path: 32 (over x, y, core), tensor: 16 (over z).
Axes of the slice: x: 4, y: 4, z: 16, core: 2. Of those that a mesh axis runs over, the one named last changes fastest.
Arguments:
- hidden_in: bfloat16 [12288, 2048], P(('path', 'tensor')), may hold values from -120 to 120
- teacher: bfloat16 [12288, 2048], P('path'), may hold values from -3 to 3
- params: bfloat16 [3, 3, 7168, 2048], P(None, None, ('tensor', 'path')), may hold values from -4 to 4
- momentum: float32 [3, 3, 7168, 2048], P(None, None, ('tensor', 'path')), may hold values from -3 to 3
- path_alive: int32 [32], replicated, may hold values from 0 to 1, as said below
- path_module: int32 [32], replicated, may hold values from 0 to 2, as said below
Outputs:
- new_params: bfloat16 [3, 3, 7168, 2048], P(None, None, ('tensor', 'path'))
- new_momentum: float32 [3, 3, 7168, 2048], P(None, None, ('tensor', 'path'))
Inputs may be any that keep to these rules, and one draw needn't show every extreme that they name: `path_alive`: at least one path is dead. `path_module`: every one of the 3 modules is used by at least one path whose path_alive entry is 1.
All inputs are finite; a program needn't handle non-finite values.
Results may differ from a plain program's by a relative error of at most 0.0047.
Values may be sent and summed in bfloat16 or wider, within the bound.
No kernel may reach another device: no remote copies, remote signals or barrier semaphores. Data moves between devices by JAX's collectives and lax.ppermute only.
A program may use at most 64 MiB of HBM per device.

v0:
```python
import math
import jax
import jax.numpy as jnp
from jax import lax
from jax.sharding import PartitionSpec as P

D = 2048
FW = 7168


def module_sums(weighting, received):
    flat = received.reshape(received.shape[0], -1)
    return lax.dot_general(
        weighting, flat, (((0,), (0,)), ((), ())), preferred_element_type=jnp.float32
    )


def per_device(hidden_in, teacher, params, momentum, path_alive, path_module):
    module_count = params.shape[0]
    block_rows = params.shape[2]
    width = params.shape[3]
    path_count = path_alive.shape[0]
    contract_last = (((1,), (1,)), ((), ()))
    contract_first = (((0,), (0,)), ((), ()))
    gate_pick = jnp.take(params[:, 0], path_module, axis=0)
    up_pick = jnp.take(params[:, 1], path_module, axis=0)
    down_pick = jnp.take(params[:, 2], path_module, axis=0)
    gate_rows, up_rows, down_rows = (
        lax.all_to_all(gate_pick, "path", split_axis=0, concat_axis=0, tiled=True),
        lax.all_to_all(up_pick, "path", split_axis=0, concat_axis=0, tiled=True),
        lax.all_to_all(down_pick, "path", split_axis=0, concat_axis=0, tiled=True),
    )
    local_rows = path_count * block_rows
    gate_rows = gate_rows.reshape(local_rows, width)
    up_rows = up_rows.reshape(local_rows, width)
    down_rows = down_rows.reshape(local_rows, width)
    rows_in = lax.all_gather(hidden_in, "tensor", axis=0, tiled=True)
    mean_sq = jnp.mean(jnp.square(rows_in.astype(jnp.float32)), axis=1, keepdims=True)
    normed = (rows_in.astype(jnp.float32) * lax.rsqrt(mean_sq + 1e-05)).astype(jnp.bfloat16)
    gate_pre = lax.dot_general(
        normed, gate_rows, contract_last, preferred_element_type=jnp.float32
    ) / math.sqrt(D)
    up_proj = lax.dot_general(
        normed, up_rows, contract_last, preferred_element_type=jnp.float32
    ) / math.sqrt(D)
    sigmoid_gate = jax.nn.sigmoid(gate_pre)
    activated = gate_pre * sigmoid_gate
    hidden = (activated * up_proj).astype(jnp.bfloat16)
    partial_out = jnp.dot(hidden, down_rows, preferred_element_type=jnp.float32) / math.sqrt(FW)
    output = lax.psum(partial_out, "tensor")
    cotangent = (4.0 * (output - teacher.astype(jnp.float32))).astype(jnp.bfloat16)
    down_delta = (
        lax.dot_general(hidden, cotangent, contract_first, preferred_element_type=jnp.float32)
        / math.sqrt(FW)
    ).astype(jnp.bfloat16)
    hidden_grad = lax.dot_general(
        cotangent, down_rows, contract_last, preferred_element_type=jnp.float32
    ) / math.sqrt(FW)
    gate_grad = (
        hidden_grad * up_proj * sigmoid_gate * (1.0 + gate_pre * (1.0 - sigmoid_gate))
    ).astype(jnp.bfloat16)
    up_grad = (hidden_grad * activated).astype(jnp.bfloat16)
    member = (path_module[:, None] == jnp.arange(module_count, dtype=jnp.int32)[None, :]).astype(
        jnp.int32
    ) * path_alive[:, None]
    weighting = member.astype(jnp.bfloat16)
    counts = jnp.sum(member, axis=0).astype(jnp.float32)
    piece_shape = (path_count, block_rows, width)
    gate_delta = (
        lax.dot_general(gate_grad, normed, contract_first, preferred_element_type=jnp.float32)
        / math.sqrt(D)
    ).astype(jnp.bfloat16)
    up_delta = (
        lax.dot_general(up_grad, normed, contract_first, preferred_element_type=jnp.float32)
        / math.sqrt(D)
    ).astype(jnp.bfloat16)
    gate_got, up_got, down_got = (
        lax.all_to_all(
            gate_delta.reshape(piece_shape), "path", split_axis=0, concat_axis=0, tiled=True
        ),
        lax.all_to_all(
            up_delta.reshape(piece_shape), "path", split_axis=0, concat_axis=0, tiled=True
        ),
        lax.all_to_all(
            down_delta.reshape(piece_shape), "path", split_axis=0, concat_axis=0, tiled=True
        ),
    )
    summed = jnp.stack(
        [
            module_sums(weighting, gate_got),
            module_sums(weighting, up_got),
            module_sums(weighting, down_got),
        ],
        axis=1,
    )
    summed = summed.reshape(module_count, 3, block_rows, width)
    mean_delta = summed / counts[:, None, None, None]
    new_momentum = 0.9 * momentum + mean_delta
    new_params = (params.astype(jnp.float32) - 0.7 * (mean_delta + 0.9 * new_momentum)).astype(
        jnp.bfloat16
    )
    return (new_params, new_momentum)


def solution(mesh):
    return jax.shard_map(
        per_device,
        mesh=mesh,
        in_specs=(
            P(("path", "tensor"), None),
            P("path", None),
            P(None, None, ("tensor", "path"), None),
            P(None, None, ("tensor", "path"), None),
            P(),
            P(),
        ),
        out_specs=(
            P(None, None, ("tensor", "path"), None),
            P(None, None, ("tensor", "path"), None),
        ),
        check_vma=False,
    )
```

profile of v0, /device:TPU:1, one launch (start us, length us, event | category | flops | bytes accessed | tf_op | source)
XLA Modules:
  0.0 420.3 jit_solution(7197902476013149992)
XLA Ops:
  10.3 2.0 gather_fusion.1
  12.4 2.0 gather_fusion.2
  14.4 4.8 %broadcast_select_fusion = (bf16[32,14,2048]{2,1,0:T(8,128)(2,1)}, bf16[32,14,2048]{2,1,0:T(8,128)(2,1)}, bf16[32,14,2048]{2,1,0:T(8,128)(2,1)S(1)}) fusion(bf16[32,14,2048]{2,1,0:T(8,128)(2,1)} %gather_fusion.2, pred[32]{0:T(512)(128)(4,1)S(1)} %compare_and_fusion, bf16[32,14,2048]{2,1,0:T(8,128)(2,1)} %gather_fusion.1, bf16[32,14,2048]{2,1,0:T(8,128)(2,1)S(1)} %gather_fusion), kind=kLoop, calls=%fused_computation.15 | loop fusion | flops 2752512 | bytes 11010080 | tf_op jit(solution)/shard_map/jit(_take)/select_n | solution.py:27
  19.2 37.7 %all_to_all.30 = bf16[32,14,2048]{2,1,0:T(8,128)(2,1)S(1)} all-to-all(bf16[32,14,2048]{2,1,0:T(8,128)(2,1)S(1)} %get-tuple-element.14), channel_id=1, replica_groups=mesh['path'=32,'tensor'=16] {'path'}, dimensions={0} | all-to-all | bytes 3670016 | tf_op jit(solution)/shard_map/all_to_all | solution.py:29
  56.9 4.5 %all-to-all-start.1 = ((bf16[32,14,2048]{2,1,0:T(8,128)(2,1)}), bf16[32,14,2048]{2,1,0:T(8,128)(2,1)}, u32[]{:S(2)}, u32[]{:S(2)}) async-start(bf16[32,14,2048]{2,1,0:T(8,128)(2,1)} %get-tuple-element.13), calls=%async_computation.1 | async-start | bytes 4194304 | tf_op jit(solution)/shard_map/all_to_all | solution.py:30
  62.2 27.6 %all-to-all-done.1 = bf16[32,14,2048]{2,1,0:T(8,128)(2,1)} async-done(((bf16[32,14,2048]{2,1,0:T(8,128)(2,1)}), bf16[32,14,2048]{2,1,0:T(8,128)(2,1)}, u32[]{:S(2)}, u32[]{:S(2)}) %all-to-all-start.1) | async-done | bytes 1835040 | tf_op jit(solution)/shard_map/all_to_all | solution.py:30
  89.9 5.2 %all-to-all-start.2 = ((bf16[32,14,2048]{2,1,0:T(8,128)(2,1)}), bf16[32,14,2048]{2,1,0:T(8,128)(2,1)}, u32[]{:S(2)}, u32[]{:S(2)}) async-start(bf16[32,14,2048]{2,1,0:T(8,128)(2,1)} %get-tuple-element.12), calls=%async_computation.2 | async-start | bytes 4194304 | tf_op jit(solution)/shard_map/all_to_all | solution.py:31
  96.6 3.7 reshape.75
  100.3 23.2 %all-to-all-done.2 = bf16[32,14,2048]{2,1,0:T(8,128)(2,1)} async-done(((bf16[32,14,2048]{2,1,0:T(8,128)(2,1)}), bf16[32,14,2048]{2,1,0:T(8,128)(2,1)}, u32[]{:S(2)}, u32[]{:S(2)}) %all-to-all-start.2) | async-done | bytes 1835040 | tf_op jit(solution)/shard_map/all_to_all | solution.py:31
  123.5 2.5 reshape.76
  126.1 4.1 all-gather.2.cloned.1.call-done
  130.2 1.8 fusion
  132.0 3.3 convolution_multiply_fusion.3
  135.4 2.1 multiply_convert_fusion.6
  138.2 2.7 convolution_multiply_fusion
  140.9 147.1 %all-reduce.2.cloned.1.call-done = f32[384,2048]{1,0:T(8,128)} async-done(((f32[384,2048]{1,0:T(8,128)}), f32[384,2048]{1,0:T(8,128)}) %all-reduce.2.cloned.1.call-update) | async-done | bytes 3145744 | tf_op jit(solution)/shard_map/psum | solution.py:50
  288.0 3.2 convolution_multiply_fusion.1
  295.1 16.8 %all-to-all-start.3 = ((bf16[32,14,2048]{2,1,0:T(8,128)(2,1)}), bf16[32,14,2048]{2,1,0:T(8,128)(2,1)}, u32[]{:S(2)}, u32[]{:S(2)}) async-start(bf16[32,14,2048]{2,1,0:T(8,128)(2,1)} %reshape.77), calls=%async_computation.3 | async-start | bytes 4194304 | tf_op jit(solution)/shard_map/all_to_all | solution.py:78
  311.9 3.1 multiply_convert_fusion.1
  315.0 1.7 reshape.80
  316.7 23.6 %all-to-all-done.3 = bf16[32,14,2048]{2,1,0:T(8,128)(2,1)} async-done(((bf16[32,14,2048]{2,1,0:T(8,128)(2,1)}), bf16[32,14,2048]{2,1,0:T(8,128)(2,1)}, u32[]{:S(2)}, u32[]{:S(2)}) %all-to-all-start.3) | async-done | bytes 1835040 | tf_op jit(solution)/shard_map/all_to_all | solution.py:78
  340.3 5.2 %all-to-all-start.4 = ((bf16[32,14,2048]{2,1,0:T(8,128)(2,1)}), bf16[32,14,2048]{2,1,0:T(8,128)(2,1)}, u32[]{:S(2)}, u32[]{:S(2)}) async-start(bf16[32,14,2048]{2,1,0:T(8,128)(2,1)} %reshape.80), calls=%async_computation.4 | async-start | bytes 4194304 | tf_op jit(solution)/shard_map/all_to_all | solution.py:81
  345.5 3.2 multiply_convert_fusion
  348.7 1.6 reshape.83
  350.3 23.7 %all-to-all-done.4 = bf16[32,14,2048]{2,1,0:T(8,128)(2,1)} async-done(((bf16[32,14,2048]{2,1,0:T(8,128)(2,1)}), bf16[32,14,2048]{2,1,0:T(8,128)(2,1)}, u32[]{:S(2)}, u32[]{:S(2)}) %all-to-all-start.4) | async-done | bytes 1835040 | tf_op jit(solution)/shard_map/all_to_all | solution.py:81
  374.0 4.5 %all-to-all-start.5 = ((bf16[32,14,2048]{2,1,0:T(8,128)(2,1)}), bf16[32,14,2048]{2,1,0:T(8,128)(2,1)S(1)}, u32[]{:S(2)}, u32[]{:S(2)}) async-start(bf16[32,14,2048]{2,1,0:T(8,128)(2,1)} %reshape.83), calls=%async_computation.5 | async-start | bytes 4194304 | tf_op jit(solution)/shard_map/all_to_all | solution.py:84
  378.6 3.6 convolution_bitcast_fusion.2
  382.2 4.4 %convolution_bitcast_fusion.1 = f32[3,1,14,2048]{3,0,2,1:T(4,128)} fusion(s32[32]{0:T(128)S(1)} %copy-done.9, s32[32]{0:T(128)S(1)} %copy-done.10, bf16[4,8,14,2048]{3,2,1,0:T(8,128)(2,1)} %bitcast.18), kind=kOutput, calls=%fused_computation.13 | convolution fusion | flops 5505312 | bytes 2179328 | tf_op jit(solution)/shard_map/dot_general | solution.py:13
  386.6 20.2 %all-to-all-done.5 = bf16[32,14,2048]{2,1,0:T(8,128)(2,1)S(1)} async-done(((bf16[32,14,2048]{2,1,0:T(8,128)(2,1)}), bf16[32,14,2048]{2,1,0:T(8,128)(2,1)S(1)}, u32[]{:S(2)}, u32[]{:S(2)}) %all-to-all-start.5) | async-done | bytes 1835040 | tf_op jit(solution)/shard_map/all_to_all | solution.py:84
  406.9 2.0 convolution_bitcast_fusion
  408.9 1.7 fusion.8
  410.7 1.6 copy.18
  (44 shorter events, 11.5 us)
Async XLA Ops:
  56.9 32.9 %all-to-all-start.1 = ((bf16[32,14,2048]{2,1,0:T(8,128)(2,1)}), bf16[32,14,2048]{2,1,0:T(8,128)(2,1)}, u32[]{:S(2)}, u32[]{:S(2)}) async-start(bf16[32,14,2048]{2,1,0:T(8,128)(2,1)} %get-tuple-element.13), calls=%async_computation.1 | async-start | bytes 4194304 | tf_op jit(solution)/shard_map/all_to_all | solution.py:30
  61.5 68.7 %all-gather.2.cloned.1.call-start = ((), (), s32[]{:S(2)}) async-start(), calls=%async_computation.6 | async-start | bytes 1671168 | tf_op jit(solution)/shard_map/all_gather | solution.py:37
  89.9 33.7 %all-to-all-start.2 = ((bf16[32,14,2048]{2,1,0:T(8,128)(2,1)}), bf16[32,14,2048]{2,1,0:T(8,128)(2,1)}, u32[]{:S(2)}, u32[]{:S(2)}) async-start(bf16[32,14,2048]{2,1,0:T(8,128)(2,1)} %get-tuple-element.12), calls=%async_computation.2 | async-start | bytes 4194304 | tf_op jit(solution)/shard_map/all_to_all | solution.py:31
  95.0 193.0 %all-reduce.2.cloned.1.call-start = ((), (), s32[]{:S(2)}) async-start(), calls=%async_computation.7 | async-start | bytes 6291456 | tf_op jit(solution)/shard_map/psum | solution.py:50
  132.0 3.4 copy-start.3
  132.0 3.4 copy-start.4
  135.3 2.1 copy-start.11
  137.4 0.7 copy-start.1
  140.9 147.2 %copy-start = (bf16[384,2048]{1,0:T(8,128)(2,1)S(1)}, bf16[384,2048]{1,0:T(8,128)(2,1)}, u32[]{:S(2)}) copy-start(bf16[384,2048]{1,0:T(8,128)(2,1)} %param.9) | copy-start | bytes 4718596
  288.0 4.1 copy-start.5
  288.0 4.1 copy-start.12
  288.0 4.1 copy-start.13
  291.2 0.9 copy-start.7
  295.1 45.2 %all-to-all-start.3 = ((bf16[32,14,2048]{2,1,0:T(8,128)(2,1)}), bf16[32,14,2048]{2,1,0:T(8,128)(2,1)}, u32[]{:S(2)}, u32[]{:S(2)}) async-start(bf16[32,14,2048]{2,1,0:T(8,128)(2,1)} %reshape.77), calls=%async_computation.3 | async-start | bytes 4194304 | tf_op jit(solution)/shard_map/all_to_all | solution.py:78
  340.3 33.6 %all-to-all-start.4 = ((bf16[32,14,2048]{2,1,0:T(8,128)(2,1)}), bf16[32,14,2048]{2,1,0:T(8,128)(2,1)}, u32[]{:S(2)}, u32[]{:S(2)}) async-start(bf16[32,14,2048]{2,1,0:T(8,128)(2,1)} %reshape.80), calls=%async_computation.4 | async-start | bytes 4194304 | tf_op jit(solution)/shard_map/all_to_all | solution.py:81
  350.3 28.2 %copy-start.9 = (s32[32]{0:T(128)S(1)}, s32[32]{0:T(128)}, u32[]{:S(2)}) copy-start(s32[32]{0:T(128)} %param.12) | copy-start | bytes 388
  350.3 28.2 %copy-start.10 = (s32[32]{0:T(128)S(1)}, s32[32]{0:T(128)}, u32[]{:S(2)}) copy-start(s32[32]{0:T(128)} %param.13) | copy-start | bytes 388
  374.0 32.9 %all-to-all-start.5 = ((bf16[32,14,2048]{2,1,0:T(8,128)(2,1)}), bf16[32,14,2048]{2,1,0:T(8,128)(2,1)S(1)}, u32[]{:S(2)}, u32[]{:S(2)}) async-start(bf16[32,14,2048]{2,1,0:T(8,128)(2,1)} %reshape.83), calls=%async_computation.5 | async-start | bytes 4194304 | tf_op jit(solution)/shard_map/all_to_all | solution.py:84
  386.6 22.3 %copy-start.2 = (bf16[3,3,14,2048]{3,2,1,0:T(8,128)(2,1)S(1)}, bf16[3,3,14,2048]{3,2,1,0:T(8,128)(2,1)}, u32[]{:S(2)}) copy-start(bf16[3,3,14,2048]{3,2,1,0:T(8,128)(2,1)} %param.10) | copy-start | bytes 1548292
  406.9 2.1 copy-start.6
  406.9 2.1 copy-start.8
Sparse Core Ops, SparseCore 0:
  64.4 65.7 all-gather.1
  141.0 146.9 all-reduce.1
where the time goes:
time: 421 us; the launch traced here: 420 us
  waiting for transfers between devices  270 us (64%)
  blocking collectives  37.7 us (9%)
  starting transfers between devices  36.3 us (9%)
  matrix products  29 us (7%)
  local copies, waits for them, and re-layouts  23 us (5%)
  between operations  14.2 us (3%)
  other arithmetic  9.82 us (2%)
    psum x1, waiting for transfers between devices, per_device(): output = lax.psum(partial_out, 'tensor')  147 us
    all_to_all x1, blocking collectives, per_device(): lax.all_to_all(gate_pick, 'path', split_axis=0, concat_axis=0, tiled=True)  37.7 us
    all_to_all x1, waiting for transfers between devices, per_device(): lax.all_to_all(up_pick, 'path', split_axis=0, concat_axis=0, tiled=True)  27.6 us
    all_to_all x1, waiting for transfers between devices, per_device(): lax.all_to_all(up_delta.reshape(piece_shape), 'path', split_axis=0, conca...  23.7 us
    all_to_all x1, waiting for transfers between devices, per_device(): lax.all_to_all(gate_delta.reshape(piece_shape), 'path', split_axis=0, con...  23.6 us
    all_to_all x1, waiting for transfers between devices, per_device(): lax.all_to_all(down_pick, 'path', split_axis=0, concat_axis=0, tiled=True)  23.2 us
    all_to_all x1, waiting for transfers between devices, per_device(): lax.all_to_all(down_delta.reshape(piece_shape), 'path', split_axis=0, con...  20.2 us
    all_to_all x1, starting transfers between devices, per_device(): lax.all_to_all(gate_delta.reshape(piece_shape), 'path', split_axis=0, con...  16.8 us
  transfers between devices with their start and end apart: 7, of which 7 were waited for; matrix products, arithmetic and copies ran while one was open for 6% of the time, Pallas kernels for 0%

commit v1 on v0

--- a/solution.py
+++ b/solution.py
@@ -6,6 +6,14 @@
 
 D = 2048
 FW = 7168
+
+
+def sum_by_hops(value, axis):
+    n_dev, total = (lax.axis_size(axis), value)
+    for hop in [1 << k for k in range(n_dev.bit_length() - 1)]:
+        swap = [(i, i ^ hop) for i in range(n_dev)]
+        total = total + lax.ppermute(total, axis, swap)
+    return total
 
 
 def module_sums(weighting, received):
@@ -47,7 +55,7 @@
     activated = gate_pre * sigmoid_gate
     hidden = (activated * up_proj).astype(jnp.bfloat16)
     partial_out = jnp.dot(hidden, down_rows, preferred_element_type=jnp.float32) / math.sqrt(FW)
-    output = lax.psum(partial_out, "tensor")
+    output = sum_by_hops(partial_out, "tensor")
     cotangent = (4.0 * (output - teacher.astype(jnp.float32))).astype(jnp.bfloat16)
     down_delta = (
         lax.dot_general(hidden, cotangent, contract_first, preferred_element_type=jnp.float32)

time: 421 us -> 1020 us (2.42)
  waiting for transfers between devices: 270 us -> 788 us
  starting transfers between devices: 36.3 us -> 117 us
    ppermute x0 -> x4, waiting for transfers between devices: none -> 668 us  [sum_by_hops(): total = total + lax.ppermute(total, axis, swap)]
    psum x1 -> x0, waiting for transfers between devices: 147 us -> none  [per_device(): output = lax.psum(partial_out, 'tensor')]
    ppermute x0 -> x4, starting transfers between devices: none -> 92 us  [sum_by_hops(): total = total + lax.ppermute(total, axis, swap)]
    all_to_all x1, starting transfers between devices: 16.8 us -> 4.95 us  [per_device(): lax.all_to_all(gate_delta.reshape(piece_shape), 'path', split_axis=0, con...]
  transfers between devices with their start and end apart: 7 -> 10, of which waited for: 7 -> 10; matrix products, arithmetic and copies ran while one was open for 6% -> 3% of each run, Pallas kernels for 0% -> 0%
where the time goes in v1:
time: 1020 us
  waiting for transfers between devices  788 us (77%)
  starting transfers between devices  117 us (11%)
  blocking collectives  37.7 us (4%)
  local copies, waits for them, and re-layouts  25.3 us (2%)
  matrix products  25.3 us (2%)
  between operations  14.3 us (1%)
  other arithmetic  12.7 us (1%)
    ppermute x4, waiting for transfers between devices, sum_by_hops(): total = total + lax.ppermute(total, axis, swap)  668 us
    ppermute x4, starting transfers between devices, sum_by_hops(): total = total + lax.ppermute(total, axis, swap)  92 us
    all_to_all x1, blocking collectives, per_device(): lax.all_to_all(gate_pick, 'path', split_axis=0, concat_axis=0, tiled=True)  37.7 us
    all_to_all x1, waiting for transfers between devices, per_device(): lax.all_to_all(up_pick, 'path', split_axis=0, concat_axis=0, tiled=True)  27.6 us
    all_to_all x1, waiting for transfers between devices, per_device(): lax.all_to_all(down_pick, 'path', split_axis=0, concat_axis=0, tiled=True)  23.3 us
    all_to_all x1, waiting for transfers between devices, per_device(): lax.all_to_all(down_delta.reshape(piece_shape), 'path', split_axis=0, con...  22.6 us
    all_to_all x1, waiting for transfers between devices, per_device(): lax.all_to_all(up_delta.reshape(piece_shape), 'path', split_axis=0, conca...  21.1 us
    all_to_all x1, waiting for transfers between devices, per_device(): lax.all_to_all(gate_delta.reshape(piece_shape), 'path', split_axis=0, con...  20.7 us
  transfers between devices with their start and end apart: 10, of which 10 were waited for; matrix products, arithmetic and copies ran while one was open for 3% of the time, Pallas kernels for 0%

profile of v1, /device:TPU:1, one launch (start us, length us, event | category | flops | bytes accessed | tf_op | source)
XLA Modules:
  0.0 1020.6 jit_solution(4684950768324377970)
XLA Ops:
  10.3 2.0 gather_fusion.1
  14.4 4.9 broadcast_select_fusion
  19.2 37.7 %all_to_all.30 = bf16[32,14,2048]{2,1,0:T(8,128)(2,1)S(1)} all-to-all(bf16[32,14,2048]{2,1,0:T(8,128)(2,1)S(1)} %get-tuple-element.14), channel_id=1, replica_groups=mesh['path'=32,'tensor'=16] {'path'}, dimensions={0} | all-to-all | bytes 3670016 | tf_op jit(solution)/shard_map/all_to_all | solution.py:37
  56.9 4.6 all-to-all-start.1
  62.2 27.6 %all-to-all-done.1 = bf16[32,14,2048]{2,1,0:T(8,128)(2,1)} async-done(((bf16[32,14,2048]{2,1,0:T(8,128)(2,1)}), bf16[32,14,2048]{2,1,0:T(8,128)(2,1)}, u32[]{:S(2)}, u32[]{:S(2)}) %all-to-all-start.1) | async-done | bytes 1835040 | tf_op jit(solution)/shard_map/all_to_all | solution.py:38
  89.9 5.2 all-to-all-start.2
  96.6 3.7 reshape.75
  100.3 23.3 %all-to-all-done.2 = bf16[32,14,2048]{2,1,0:T(8,128)(2,1)} async-done(((bf16[32,14,2048]{2,1,0:T(8,128)(2,1)}), bf16[32,14,2048]{2,1,0:T(8,128)(2,1)}, u32[]{:S(2)}, u32[]{:S(2)}) %all-to-all-start.2) | async-done | bytes 1835040 | tf_op jit(solution)/shard_map/all_to_all | solution.py:39
  123.5 2.5 reshape.76
  126.1 4.1 all-gather.2.cloned.1.call-done
  132.0 3.3 convolution_multiply_fusion.3
  137.6 2.7 collective-permute-start
  140.3 59.3 %collective-permute-done = f32[384,2048]{1,0:T(8,128)S(1)} collective-permute-done((f32[384,2048]{1,0:T(8,128)S(1)}, f32[384,2048]{1,0:T(8,128)S(1)}, u32[]{:S(2)}, u32[]{:S(2)}) %collective-permute-start) | collective-permute-done | bytes 3145760 | tf_op jit(solution)/shard_map/ppermute | solution.py:15
  200.3 3.2 collective-permute-start.1
  203.6 132.2 %collective-permute-done.1 = f32[384,2048]{1,0:T(8,128)S(1)} collective-permute-done((f32[384,2048]{1,0:T(8,128)S(1)}, f32[384,2048]{1,0:T(8,128)S(1)}, u32[]{:S(2)}, u32[]{:S(2)}) %collective-permute-start.1) | collective-permute-done | bytes 3145760 | tf_op jit(solution)/shard_map/ppermute | solution.py:15
  336.5 4.0 collective-permute-start.2
  340.4 341.1 %collective-permute-done.2 = f32[384,2048]{1,0:T(8,128)S(1)} collective-permute-done((f32[384,2048]{1,0:T(8,128)S(1)}, f32[384,2048]{1,0:T(8,128)S(1)}, u32[]{:S(2)}, u32[]{:S(2)}) %collective-permute-start.2) | collective-permute-done | bytes 3145760 | tf_op jit(solution)/shard_map/ppermute | solution.py:15
  682.3 82.1 %collective-permute-start.3 = (f32[384,2048]{1,0:T(8,128)S(1)}, f32[384,2048]{1,0:T(8,128)S(1)}, u32[]{:S(2)}, u32[]{:S(2)}) collective-permute-start(f32[384,2048]{1,0:T(8,128)S(1)} %add.46), channel_id=1, source_target_pairs={{0,8},{1,9},{2,10},{3,11},{4,12},{5,13},{6,14},{7,15},{8,0},{9,1},... | collective-permute-start | bytes 9437192 | tf_op jit(solution)/shard_map/ppermute | solution.py:15
  764.4 135.4 %collective-permute-done.3 = f32[384,2048]{1,0:T(8,128)S(1)} collective-permute-done((f32[384,2048]{1,0:T(8,128)S(1)}, f32[384,2048]{1,0:T(8,128)S(1)}, u32[]{:S(2)}, u32[]{:S(2)}) %collective-permute-start.3) | collective-permute-done | bytes 3145760 | tf_op jit(solution)/shard_map/ppermute | solution.py:15
  904.9 4.9 all-to-all-start.3
  909.8 4.1 multiply_convert_fusion.1
  913.9 3.6 reshape.80
  917.5 20.7 %all-to-all-done.3 = bf16[32,14,2048]{2,1,0:T(8,128)(2,1)S(1)} async-done(((bf16[32,14,2048]{2,1,0:T(8,128)(2,1)}), bf16[32,14,2048]{2,1,0:T(8,128)(2,1)S(1)}, u32[]{:S(2)}, u32[]{:S(2)}) %all-to-all-start.3) | async-done | bytes 1835040 | tf_op jit(solution)/shard_map/all_to_all | solution.py:86
  938.2 5.2 all-to-all-start.4
  943.4 3.8 multiply_convert_fusion
  947.2 3.6 reshape.83
  950.8 21.1 %all-to-all-done.4 = bf16[32,14,2048]{2,1,0:T(8,128)(2,1)} async-done(((bf16[32,14,2048]{2,1,0:T(8,128)(2,1)}), bf16[32,14,2048]{2,1,0:T(8,128)(2,1)}, u32[]{:S(2)}, u32[]{:S(2)}) %all-to-all-start.4) | async-done | bytes 1835040 | tf_op jit(solution)/shard_map/all_to_all | solution.py:89
  971.9 5.2 all-to-all-start.5
  977.2 2.0 convolution_bitcast_fusion.2
  979.3 3.6 convolution_bitcast_fusion.1
  982.9 22.6 %all-to-all-done.5 = bf16[32,14,2048]{2,1,0:T(8,128)(2,1)} async-done(((bf16[32,14,2048]{2,1,0:T(8,128)(2,1)}), bf16[32,14,2048]{2,1,0:T(8,128)(2,1)}, u32[]{:S(2)}, u32[]{:S(2)}) %all-to-all-start.5) | async-done | bytes 1835040 | tf_op jit(solution)/shard_map/all_to_all | solution.py:92
  1005.5 3.6 convolution_bitcast_fusion
  (43 shorter events, 23.2 us)
Async XLA Ops:
  56.9 32.9 %all-to-all-start.1 = ((bf16[32,14,2048]{2,1,0:T(8,128)(2,1)}), bf16[32,14,2048]{2,1,0:T(8,128)(2,1)}, u32[]{:S(2)}, u32[]{:S(2)}) async-start(bf16[32,14,2048]{2,1,0:T(8,128)(2,1)} %get-tuple-element.13), calls=%async_computation.1 | async-start | bytes 4194304 | tf_op jit(solution)/shard_map/all_to_all | solution.py:38
  61.5 68.7 %all-gather.2.cloned.1.call-start = ((), (), s32[]{:S(2)}) async-start(), calls=%async_computation.6 | async-start | bytes 1671168 | tf_op jit(solution)/shard_map/all_gather | solution.py:45
  89.9 33.7 %all-to-all-start.2 = ((bf16[32,14,2048]{2,1,0:T(8,128)(2,1)}), bf16[32,14,2048]{2,1,0:T(8,128)(2,1)}, u32[]{:S(2)}, u32[]{:S(2)}) async-start(bf16[32,14,2048]{2,1,0:T(8,128)(2,1)} %get-tuple-element.12), calls=%async_computation.2 | async-start | bytes 4194304 | tf_op jit(solution)/shard_map/all_to_all | solution.py:39
  132.0 3.4 copy-start.1
  132.0 3.4 copy-start.4
  135.4 766.5 %copy-start.8 = (f32[384,448]{0,1:T(8,128)}, f32[384,448]{0,1:T(8,128)S(1)}, u32[]{:S(2)}) copy-start(f32[384,448]{0,1:T(8,128)S(1)} %convolution_multiply_fusion.3) | copy-start | bytes 2064388
  137.6 62.0 %collective-permute-start = (f32[384,2048]{1,0:T(8,128)S(1)}, f32[384,2048]{1,0:T(8,128)S(1)}, u32[]{:S(2)}, u32[]{:S(2)}) collective-permute-start(f32[384,2048]{1,0:T(8,128)S(1)} %convolution_multiply_fusion), channel_id=1, source_target_pairs={{0,1},{1,0},{2,3},{3,2},{4,5},{5,4},{6,7},{7,6},{8,9},{9,8},{10,11... | collective-permute-start | bytes 9437192 | tf_op jit(solution)/shard_map/ppermute | solution.py:15
  200.3 135.4 %collective-permute-start.1 = (f32[384,2048]{1,0:T(8,128)S(1)}, f32[384,2048]{1,0:T(8,128)S(1)}, u32[]{:S(2)}, u32[]{:S(2)}) collective-permute-start(f32[384,2048]{1,0:T(8,128)S(1)} %add.44), channel_id=1, source_target_pairs={{0,2},{1,3},{2,0},{3,1},{4,6},{5,7},{6,4},{7,5},{8,10},{9,11},{10,... | collective-permute-start | bytes 9437192 | tf_op jit(solution)/shard_map/ppermute | solution.py:15
  336.5 563.3 %copy-start.2 = (bf16[384,2048]{1,0:T(8,128)(2,1)S(1)}, bf16[384,2048]{1,0:T(8,128)(2,1)}, u32[]{:S(2)}) copy-start(bf16[384,2048]{1,0:T(8,128)(2,1)} %param.9) | copy-start | bytes 4718596
  336.5 345.1 %collective-permute-start.2 = (f32[384,2048]{1,0:T(8,128)S(1)}, f32[384,2048]{1,0:T(8,128)S(1)}, u32[]{:S(2)}, u32[]{:S(2)}) collective-permute-start(f32[384,2048]{1,0:T(8,128)S(1)} %add.45), channel_id=1, source_target_pairs={{0,4},{1,5},{2,6},{3,7},{4,0},{5,1},{6,2},{7,3},{8,12},{9,13},{10,... | collective-permute-start | bytes 9437192 | tf_op jit(solution)/shard_map/ppermute | solution.py:15
  682.3 217.5 %collective-permute-start.3 = (f32[384,2048]{1,0:T(8,128)S(1)}, f32[384,2048]{1,0:T(8,128)S(1)}, u32[]{:S(2)}, u32[]{:S(2)}) collective-permute-start(f32[384,2048]{1,0:T(8,128)S(1)} %add.46), channel_id=1, source_target_pairs={{0,8},{1,9},{2,10},{3,11},{4,12},{5,13},{6,14},{7,15},{8,0},{9,1},... | collective-permute-start | bytes 9437192 | tf_op jit(solution)/shard_map/ppermute | solution.py:15
  900.7 1.2 copy-start.3
  904.9 33.4 %all-to-all-start.3 = ((bf16[32,14,2048]{2,1,0:T(8,128)(2,1)}), bf16[32,14,2048]{2,1,0:T(8,128)(2,1)S(1)}, u32[]{:S(2)}, u32[]{:S(2)}) async-start(bf16[32,14,2048]{2,1,0:T(8,128)(2,1)} %reshape.77), calls=%async_computation.3 | async-start | bytes 4194304 | tf_op jit(solution)/shard_map/all_to_all | solution.py:86
  938.2 33.7 %all-to-all-start.4 = ((bf16[32,14,2048]{2,1,0:T(8,128)(2,1)}), bf16[32,14,2048]{2,1,0:T(8,128)(2,1)}, u32[]{:S(2)}, u32[]{:S(2)}) async-start(bf16[32,14,2048]{2,1,0:T(8,128)(2,1)} %reshape.80), calls=%async_computation.4 | async-start | bytes 4194304 | tf_op jit(solution)/shard_map/all_to_all | solution.py:89
  950.8 26.3 %copy-start.6 = (s32[32]{0:T(128)S(1)}, s32[32]{0:T(128)}, u32[]{:S(2)}) copy-start(s32[32]{0:T(128)} %param.12) | copy-start | bytes 388
  950.8 26.3 %copy-start.7 = (s32[32]{0:T(128)S(1)}, s32[32]{0:T(128)}, u32[]{:S(2)}) copy-start(s32[32]{0:T(128)} %param.13) | copy-start | bytes 388
  971.9 33.7 %all-to-all-start.5 = ((bf16[32,14,2048]{2,1,0:T(8,128)(2,1)}), bf16[32,14,2048]{2,1,0:T(8,128)(2,1)}, u32[]{:S(2)}, u32[]{:S(2)}) async-start(bf16[32,14,2048]{2,1,0:T(8,128)(2,1)} %reshape.83), calls=%async_computation.5 | async-start | bytes 4194304 | tf_op jit(solution)/shard_map/all_to_all | solution.py:92
  982.9 26.3 %copy-start = (bf16[3,3,14,2048]{3,2,1,0:T(8,128)(2,1)S(1)}, bf16[3,3,14,2048]{3,2,1,0:T(8,128)(2,1)}, u32[]{:S(2)}) copy-start(bf16[3,3,14,2048]{3,2,1,0:T(8,128)(2,1)} %param.10) | copy-start | bytes 1548292
  982.9 26.3 %copy-start.5 = (f32[3,3,14,2048]{3,2,1,0:T(8,128)S(1)}, f32[3,3,14,2048]{3,2,1,0:T(8,128)}, u32[]{:S(2)}) copy-start(f32[3,3,14,2048]{3,2,1,0:T(8,128)} %param.11) | copy-start | bytes 3096580
Sparse Core Ops, SparseCore 0:
  64.4 65.7 all-gather.1
